TPU v7x, 512 devices: a whole 4x4x16 slice. The times are simulated.
512 devices in a mesh: fibre: 128 (over x, y_hi, z), seg: 4 (over y_lo, core).
Axes of the slice: x: 4, y: 4 (y_hi: 2, y_lo: 2; y = y_hi * 2 + y_lo), z: 16, core: 2. Of those that a mesh axis runs over, the one named last changes fastest.
Arguments:
- data: bfloat16 [4, 1024, 2048], P('seg', 'fibre')
- sources: int32 [2, 4], replicated, may hold values from 0 to 7
- owners: int32 [2], replicated, may hold values from 0 to 127
Outputs:
- correlations: float32 [2, 4, 1024, 1024], P(None, None, ('fibre', 'seg'))
All inputs are finite; a program needn't handle non-finite values.
Results may differ from a plain program's by a relative error of at most 0.0066.
Values may be sent and summed in bfloat16 or wider, within the bound.
No kernel may reach another device: no remote copies, remote signals or barrier semaphores. Data moves between devices by JAX's collectives and lax.ppermute only.
A program may use at most 64 MiB of HBM per device.

v0:
```python
import math
import jax
import jax.numpy as jnp
from jax import lax
from jax.sharding import PartitionSpec as P

BAND = 128
LAGS = 1024


def spread(block, axis, holder):
    block = jnp.where(lax.axis_index(axis) == holder, block, jnp.zeros_like(block))
    return lax.psum(block, axis)


def extended(cells, sides, width):
    for axis, dim in sides:
        count = lax.axis_size(axis)
        ends = count - 1
        head = lax.slice_in_dim(cells, 0, width, axis=dim)
        tail = lax.slice_in_dim(cells, cells.shape[dim] - width, cells.shape[dim], axis=dim)
        cells = jnp.concatenate(
            [
                lax.ppermute(tail, axis, [(i, (i + 1) % count) for i in range(ends)]),
                cells,
                lax.ppermute(head, axis, [((i + 1) % count, i) for i in range(ends)]),
            ],
            axis=dim,
        )
    return cells


def make_tables(length, lags):
    half = length // 2
    times = jnp.arange(length, dtype=jnp.int32)
    freqs = jnp.arange(half, dtype=jnp.int32)
    phase = times[:, None] * freqs[None, :] % length
    angle = phase.astype(jnp.float32) * (2.0 * math.pi / length)
    forward = jnp.concatenate([jnp.cos(angle), -jnp.sin(angle)], axis=1).astype(jnp.bfloat16)
    shifts = jnp.arange(lags, dtype=jnp.int32) - lags // 2 + length
    phase_back = freqs[:, None] * shifts[None, :] % length
    angle_back = phase_back.astype(jnp.float32) * (2.0 * math.pi / length)
    inverse = jnp.concatenate([jnp.cos(angle_back), -jnp.sin(angle_back)], axis=0) * (
        1.0 / math.sqrt(half)
    )
    return (forward, inverse)


def whiten(spectra, band):
    lead = spectra.shape[:-1]
    width = spectra.shape[-1] // 2
    parts = spectra.reshape(lead + (2, width // band, band))
    power = jnp.sum(parts * parts, axis=(-3, -1)) / (2.0 * band)
    scale = lax.rsqrt(power + 1e-06)
    return (parts * scale[..., None, :, None]).reshape(spectra.shape)


def cross_sum(receivers, emitters):
    half = receivers.shape[2] // 2
    rec_re, rec_im = (receivers[..., :half], receivers[..., half:])
    emi_re, emi_im = (emitters[..., :half], emitters[..., half:])
    real_part = jnp.einsum("sck,snk->nck", rec_re, emi_re, preferred_element_type=jnp.float32)
    real_part = real_part + jnp.einsum(
        "sck,snk->nck", rec_im, emi_im, preferred_element_type=jnp.float32
    )
    imag_part = jnp.einsum("sck,snk->nck", rec_im, emi_re, preferred_element_type=jnp.float32)
    imag_part = imag_part - jnp.einsum(
        "sck,snk->nck", rec_re, emi_im, preferred_element_type=jnp.float32
    )
    return jnp.concatenate([real_part, imag_part], axis=-1)


def correlate(cross, inverse):
    count, chans, width = cross.shape
    flat = jnp.dot(cross.reshape(count * chans, width), inverse, precision=lax.Precision.HIGHEST)
    return flat.reshape(count, chans, inverse.shape[1])


def shards(data, sources, owners):
    seg_dev, ch_dev, length = data.shape
    steps = sources.shape[0]
    forward, inverse = make_tables(length, LAGS)
    spectra = jnp.dot(
        data.reshape(seg_dev * ch_dev, length), forward, preferred_element_type=jnp.float32
    )
    white = whiten(spectra.reshape(seg_dev, ch_dev, length), BAND).astype(jnp.bfloat16)
    selector = (sources[:, :, None] == jnp.arange(ch_dev, dtype=jnp.int32)[None, None, :]).astype(
        jnp.bfloat16
    )
    picked = jnp.einsum("pnc,scf->psnf", selector, white, preferred_element_type=jnp.float32)
    received = []
    for step in range(steps):
        received.append(spread(picked[step].astype(jnp.bfloat16), "fibre", owners[step]))
    chosen = jnp.stack(received)
    padded = extended(white, (("fibre", 1),), 4)
    total = padded[:, 0:ch_dev].astype(jnp.float32)
    for offset in range(1, 8):
        total = total + padded[:, offset : offset + ch_dev].astype(jnp.float32)
    stacked = (total * 0.125).astype(jnp.bfloat16)
    partial_list = [correlate(cross_sum(stacked, chosen[step]), inverse) for step in range(steps)]
    return lax.psum_scatter(jnp.stack(partial_list), "seg", scatter_dimension=2, tiled=True)


def solution(mesh):
    return jax.shard_map(
        shards,
        mesh=mesh,
        in_specs=(P("seg", "fibre", None), P(), P()),
        out_specs=P(None, None, ("fibre", "seg"), None),
        check_vma=False,
    )
```

profile of v0, /device:TPU:1, one launch (start us, length us, event | category | flops | bytes accessed | tf_op | source)
XLA Modules:
  0.0 840.4 jit_solution(10892744764179894782)
XLA Ops:
  6.5 0.0 copy-start
  6.5 0.0 all-reduce.4.cloned.1.call-start
  6.5 33.8 %negate_convert_fusion = (bf16[2048,1024]{1,0:T(8,128)(2,1)S(1)}, bf16[2048,1024]{1,0:T(8,128)(2,1)S(1)}) fusion(), kind=kLoop, calls=%fused_computation.12 | loop fusion | flops 35651584 | bytes 8388608 | tf_op jit(solution)/shard_map/convert.44
  40.4 0.0 copy-done
  40.4 0.0 copy-start.2
  40.4 0.0 copy-start.1
  40.4 1.2 fusion.57
  41.6 0.1 reduce_sum.9
  41.7 0.1 mul.100
  41.8 4.4 collective-permute-start
  46.2 1.3 collective-permute-start.1
  47.5 0.0 copy-done.2
  47.5 0.2 fusion.26
  47.8 0.0 copy-done.1
  47.8 0.6 fusion.56
  49.7 604.6 %all-reduce.1 = (bf16[1,4,2048]{2,1,0:T(4,128)(2,1)S(1)}, bf16[1,4,2048]{2,1,0:T(4,128)(2,1)S(1)}) all-reduce(bf16[1,4,2048]{2,1,0:T(4,128)(2,1)S(1)} %get-tuple-element.18, bf16[1,4,2048]{2,1,0:T(4,128)(2,1)S(1)} %get-tuple-element.17), channel_id=1, replica_groups=mesh['fibre'=128,'seg'=4] {'fibre'}, use_global_device_ids=true, to_apply=%region_2.3 | all-reduce | flops 16384 | bytes 65536 | tf_op jit(solution)/shard_map/psum | solution.py:13
  654.3 16.7 %fusion.27 = (f32[1024,1024]{1,0:T(8,128)S(1)}, f32[1024,1024]{1,0:T(8,128)S(1)}) fusion(s32[1024]{0:T(1024)S(1)} %iota_add_fusion), kind=kLoop, calls=%fused_computation.34 | loop fusion | flops 15728640 | bytes 8392704 | tf_op jit(solution)/shard_map/cos | solution.py:43
  671.0 0.0 collective-permute-done
  671.0 0.0 collective-permute-done.1
  671.0 0.1 multiply_convert_fusion
  671.1 0.1 add_bitcast_fusion.1
  671.2 5.0 fusion.28
  676.2 5.0 fusion.31
  681.3 0.9 copy.4
  682.2 0.0 all-reduce.4.cloned.1.call-update
  682.2 1.3 dynamic-slice
  684.1 148.0 %all-reduce.4.cloned.1.call-done = f32[2,4,8,1024]{3,1,0,2:T(4,128)} async-done(((f32[2,4,8,1024]{3,1,0,2:T(4,128)}), f32[2,4,8,1024]{3,1,0,2:T(4,128)}) %all-reduce.4.cloned.1.call-update) | async-done | bytes 262160
  832.1 0.8 constant_dynamic-slice_fusion
  832.9 0.7 copy.5
  (9 shorter events, 0.1 us)
Async XLA Ops:
  6.5 33.9 %copy-start = (bf16[1,8,2048]{2,1,0:T(8,128)(2,1)S(1)}, bf16[1,8,2048]{2,1,0:T(8,128)(2,1)}, u32[]{:S(2)}) copy-start(bf16[1,8,2048]{2,1,0:T(8,128)(2,1)} %param.3) | copy-start | bytes 98308
  6.5 825.5 %all-reduce.4.cloned.1.call-start = ((), (), s32[]{:S(2)}) async-start(), calls=%async_computation | async-start | bytes 524288
  40.4 7.1 copy-start.2
  40.4 7.3 copy-start.1
  41.8 629.2 %collective-permute-start = (bf16[1,4,2048]{2,1,0:T(4,128)(2,1)S(1)}, bf16[1,4,2048]{2,1,0:T(4,128)(2,1)S(1)}, u32[]{:S(2)}, u32[]{:S(2)}) collective-permute-start(bf16[1,4,2048]{2,1,0:T(4,128)(2,1)S(1)} %get-tuple-element.15), channel_id=1, source_target_pairs={{0,4},{4,8},{8,12},{12,16},{16,20},{20,24},{24,28},{28,32},{32,36}... | collective-permute-start | bytes 49160 | tf_op jit(solution)/shard_map/ppermute | solution.py:24
  46.2 624.8 %collective-permute-start.1 = (bf16[1,4,2048]{2,1,0:T(4,128)(2,1)S(1)}, bf16[1,4,2048]{2,1,0:T(4,128)(2,1)S(1)}, u32[]{:S(2)}, u32[]{:S(2)}) collective-permute-start(bf16[1,4,2048]{2,1,0:T(4,128)(2,1)S(1)} %get-tuple-element.16), channel_id=1, source_target_pairs={{4,0},{8,4},{12,8},{16,12},{20,16},{24,20},{28,24},{32,28},{36,32}... | collective-permute-start | bytes 49160 | tf_op jit(solution)/shard_map/ppermute | solution.py:26
Sparse Core Ops, SparseCore 0:
  682.3 149.7 all-reduce.3
where the time goes:
time: 841 us; the launch traced here: 840 us
  blocking collectives  605 us (72%)
  waiting for transfers between devices  148 us (18%)
  other arithmetic  50.9 us (6%)
  between operations  15.5 us (2%)
  matrix products  11.4 us (1%)
    psum x1, blocking collectives, spread(): return lax.psum(block, axis)  605 us
    unnamed x2, waiting for transfers between devices  148 us
    another operation x4, other arithmetic  33.9 us
  transfers between devices with their start and end apart: 3, of which 1 were waited for; matrix products, arithmetic and copies ran while one was open for 2% of the time, Pallas kernels for 0%

commit v1 on v0

--- a/solution.py
+++ b/solution.py
@@ -10,7 +10,7 @@
 
 def spread(block, axis, holder):
     block = jnp.where(lax.axis_index(axis) == holder, block, jnp.zeros_like(block))
-    return lax.psum(block, axis)
+    return jnp.sum(lax.all_gather(block, axis), axis=0)
 
 
 def extended(cells, sides, width):

time: 841 us -> 543 us (0.65)
  blocking collectives: 605 us -> 0 us
  waiting for transfers between devices: 148 us -> 446 us
    psum x1 -> x0, blocking collectives: 605 us -> none  [spread(): return lax.psum(block, axis)]
    all_gather x0 -> x2, waiting for transfers between devices: none -> 392 us  [spread(): return jnp.sum(lax.all_gather(block, axis), axis=0)]
    unnamed x2 -> x4, waiting for transfers between devices: 148 us -> 54.2 us
  transfers between devices with their start and end apart: 3 -> 5, of which waited for: 1 -> 3; matrix products, arithmetic and copies ran while one was open for 2% -> 4% of each run, Pallas kernels for 0% -> 0%
where the time goes in v1:
time: 543 us
  waiting for transfers between devices  446 us (82%)
  other arithmetic  57.8 us (11%)
  between operations  15.2 us (3%)
  matrix products  13.9 us (3%)
  starting transfers between devices  5.92 us (1%)
    all_gather x2, waiting for transfers between devices, spread(): return jnp.sum(lax.all_gather(block, axis), axis=0)  392 us
    unnamed x4, waiting for transfers between devices  54.2 us
    another operation x4, other arithmetic  33.9 us
    cos x1, other arithmetic, make_tables(): jnp.cos(angle_back)  18.1 us
    dot_general x2, matrix products, correlate(): jnp.dot(cross.reshape(count * chans, width), inverse, precision=lax.Preci...  12.5 us
  transfers between devices with their start and end apart: 5, of which 3 were waited for; matrix products, arithmetic and copies ran while one was open for 4% of the time, Pallas kernels for 0%

profile of v1, /device:TPU:1, one launch (start us, length us, event | category | flops | bytes accessed | tf_op | source)
XLA Modules:
  0.0 543.2 jit_solution(9553194908825855386)
XLA Ops:
  6.5 33.8 %negate_convert_fusion = (bf16[2048,1024]{1,0:T(8,128)(2,1)S(1)}, bf16[2048,1024]{1,0:T(8,128)(2,1)S(1)}) fusion(), kind=kLoop, calls=%fused_computation.12 | loop fusion | flops 35651584 | bytes 8388608 | tf_op jit(solution)/shard_map/convert.46
  40.4 0.0 copy-start.3
  40.4 0.0 copy-start.4
  40.4 1.2 fusion.57
  41.6 0.1 reduce_sum.37
  41.7 0.6 fusion.56
  43.6 0.1 mul.100
  43.7 0.2 fusion.26
  43.9 0.6 fusion.48
  44.6 0.0 all-gather.3.cloned.1.call-update
  44.6 0.0 all-gather.5.cloned.1.call-start
  44.7 0.7 all-gather.5.cloned.1.call-update
  45.4 0.0 all-reduce.3.cloned.1.call-start
  45.4 4.4 collective-permute-start
  49.8 1.5 collective-permute-start.1
  51.3 18.1 %fusion.27 = (f32[1024,1024]{1,0:T(8,128)}, f32[1024,1024]{1,0:T(8,128)}) fusion(s32[1024]{0:T(1024)S(1)} %iota_add_fusion), kind=kLoop, calls=%fused_computation.34 | loop fusion | flops 15728640 | bytes 8392704 | tf_op jit(solution)/shard_map/cos | solution.py:43
  69.3 0.0 collective-permute-done
  69.4 0.0 collective-permute-done.1
  69.4 0.1 multiply_convert_fusion
  69.5 183.5 %all-gather.3.cloned.1.call-done = bf16[128,1,4,2048]{3,2,1,0:T(4,128)(2,1)} async-done(((bf16[1,1,4,2048]{3,2,1,0:T(4,128)(2,1)}), bf16[128,1,4,2048]{3,2,1,0:T(4,128)(2,1)}) %all-gather.3.cloned.1.call-update) | async-done | bytes 2097168 | tf_op jit(solution)/shard_map/all_gather | solution.py:13
  253.0 2.5 reduce_sum.38
  255.5 208.1 %all-gather.5.cloned.1.call-done = bf16[128,1,4,2048]{3,2,1,0:T(4,128)(2,1)} async-done(((bf16[1,1,4,2048]{3,2,1,0:T(4,128)(2,1)}), bf16[128,1,4,2048]{3,2,1,0:T(4,128)(2,1)}) %all-gather.5.cloned.1.call-update) | async-done | bytes 2097168 | tf_op jit(solution)/shard_map/all_gather | solution.py:13
  463.6 2.5 reduce_sum.40
  466.1 0.1 add_bitcast_fusion.1
  466.2 7.5 %fusion.28 = f32[1,4,8,1024]{3,2,1,0:T(8,128)S(1)} fusion(f32[1024,1024]{1,0:T(8,128)} %get-tuple-element.22, f32[1024,1024]{1,0:T(8,128)} %get-tuple-element.21, f32[4,8,1024]{2,1,0:T(8,128)S(1)} %get-tuple-element.6, f32[4,8,1024]{2,1,0:T(8,128)S(1)} %get-tuple-element.5), kind=kOutput, calls=%fused_computation.35 | convolution fusion | flops 809566208 | bytes 8781824 | tf_op jit(solution)/shard_map/dot_general | solution.py:75
  473.8 5.0 fusion.31
  478.8 0.9 copy.6
  479.7 0.0 all-reduce.3.cloned.1.call-update
  479.7 1.3 dynamic-slice
  481.6 53.5 %all-reduce.3.cloned.1.call-done = f32[2,4,8,1024]{3,1,0,2:T(4,128)} async-done(((f32[2,4,8,1024]{3,1,0,2:T(4,128)}), f32[2,4,8,1024]{3,1,0,2:T(4,128)}) %all-reduce.3.cloned.1.call-update) | async-done | bytes 262160
  535.1 0.8 constant_dynamic-slice_fusion
  536.0 0.7 copy.7
  (17 shorter events, 0.1 us)
Async XLA Ops:
  6.5 33.9 %copy-start = (bf16[1,8,2048]{2,1,0:T(8,128)(2,1)S(1)}, bf16[1,8,2048]{2,1,0:T(8,128)(2,1)}, u32[]{:S(2)}) copy-start(bf16[1,8,2048]{2,1,0:T(8,128)(2,1)} %param.3) | copy-start | bytes 98308
  6.5 246.5 %all-gather.3.cloned.1.call-start = ((), (), s32[]{:S(2)}) async-start(), calls=%async_computation | async-start | bytes 2113536 | tf_op jit(solution)/shard_map/all_gather | solution.py:13
  40.4 1.3 copy-start.3
  40.4 3.3 copy-start.4
  44.6 419.0 %all-gather.5.cloned.1.call-start = ((), (), s32[]{:S(2)}) async-start(), calls=%async_computation.1 | async-start | bytes 2113536 | tf_op jit(solution)/shard_map/all_gather | solution.py:13
  45.4 489.8 %all-reduce.3.cloned.1.call-start = ((), (), s32[]{:S(2)}) async-start(), calls=%async_computation.2 | async-start | bytes 524288
  45.4 23.9 %collective-permute-start = (bf16[1,4,2048]{2,1,0:T(4,128)(2,1)S(1)}, bf16[1,4,2048]{2,1,0:T(4,128)(2,1)S(1)}, u32[]{:S(2)}, u32[]{:S(2)}) collective-permute-start(bf16[1,4,2048]{2,1,0:T(4,128)(2,1)S(1)} %get-tuple-element.15), channel_id=1, source_target_pairs={{0,4},{4,8},{8,12},{12,16},{16,20},{20,24},{24,28},{28,32},{32,36}... | collective-permute-start | bytes 49160 | tf_op jit(solution)/shard_map/ppermute | solution.py:24
  49.8 19.6 %collective-permute-start.1 = (bf16[1,4,2048]{2,1,0:T(4,128)(2,1)S(1)}, bf16[1,4,2048]{2,1,0:T(4,128)(2,1)S(1)}, u32[]{:S(2)}, u32[]{:S(2)}) collective-permute-start(bf16[1,4,2048]{2,1,0:T(4,128)(2,1)S(1)} %get-tuple-element.16), channel_id=1, source_target_pairs={{4,0},{8,4},{12,8},{16,12},{20,16},{24,20},{28,24},{32,28},{36,32}... | collective-permute-start | bytes 49160 | tf_op jit(solution)/shard_map/ppermute | solution.py:26
  466.2 7.5 %copy-start.1 = (f32[1024,1024]{1,0:T(8,128)S(1)}, f32[1024,1024]{1,0:T(8,128)}, u32[]{:S(2)}) copy-start(f32[1024,1024]{1,0:T(8,128)} %get-tuple-element.21) | copy-start | bytes 12582916
  466.2 7.5 %copy-start.2 = (f32[1024,1024]{1,0:T(8,128)S(1)}, f32[1024,1024]{1,0:T(8,128)}, u32[]{:S(2)}) copy-start(f32[1024,1024]{1,0:T(8,128)} %get-tuple-element.22) | copy-start | bytes 12582916
Sparse Core Ops, SparseCore 0:
  44.7 208.2 all-gather.2
  257.4 206.2 all-gather.4
  479.8 55.2 all-reduce.2
